TPU v7x, 256 devices: a whole 4x4x8 slice. The times are simulated.
256 devices in a mesh: dom: 64 (over z, x, core), sub: 4 (over y).
Axes of the slice: x: 4, y: 4, z: 8, core: 2. Of those that a mesh axis runs over, the one named last changes fastest.
Arguments:
- excitation: bfloat16 [64, 1536, 64], P('dom', 'sub'), may hold values from -6 to 6
- local_inverse: bfloat16 [64, 1536, 1536], P('dom', 'sub'), as said below
- aggregation: bfloat16 [64, 1024, 1536], P('dom', None, 'sub'), may hold values from -0.15625 to 0.15625
- disaggregation: bfloat16 [64, 1536, 1024], P('dom', 'sub'), may hold values from -0.1875 to 0.1875
- translation: float32 [64, 6, 2, 512], P('dom'), may hold values from -1.5 to 1.5
- partners: int32 [64, 6], P('dom'), may hold values from 0 to 63, as said below
- list_counts: int32 [64], P('dom'), may hold values from 2 to 6
- sweep_order: int32 [64], replicated, may hold values from 0 to 63, as said below
Outputs:
- currents: float32 [64, 1536, 64], P('dom', 'sub')
Inputs may be any that keep to these rules, and one draw needn't show every extreme that they name: `partners`: row d names 6 different subdomains, none equal to d; only its first list_counts[d] slots are used. `local_inverse`: each subdomain's matrix is the identity plus independent entries of spread 0.6 / sqrt(1536). `sweep_order`: every subdomain has a position of its own.
All inputs are finite; a program needn't handle non-finite values.
Results may differ from a plain program's by a relative error of at most 0.03.
Values may be sent and summed in bfloat16 or wider, within the bound.
No kernel may reach another device: no remote copies, remote signals or barrier semaphores. Data moves between devices by JAX's collectives and lax.ppermute only.
A program may use at most 64 MiB of HBM per device.

v0:
```python
import jax
import jax.numpy as jnp
from jax import lax
from jax.sharding import PartitionSpec as P

SEGMENTS = 8
CONTRACT_FIRST = (((0,), (1,)), ((), ()))
CONTRACT_LAST = (((1,), (1,)), ((), ()))


def rotate(real_weight, imag_weight, pattern):
    samples = real_weight.shape[-1]
    values = pattern.astype(jnp.float32)
    real_part = values[..., :samples]
    imag_part = values[..., samples:]
    return jnp.concatenate(
        [
            real_weight * real_part - imag_weight * imag_part,
            real_weight * imag_part + imag_weight * real_part,
        ],
        axis=-1,
    )


def local(
    excitation,
    local_inverse,
    aggregation,
    disaggregation,
    translation,
    partners,
    list_counts,
    sweep_order,
):
    excite_rows = excitation[0]
    inverse_rows = local_inverse[0]
    agg_columns = aggregation[0]
    disagg_rows = disaggregation[0]
    trans_rows = translation[0]
    partner_row = partners[0]

    def apply_inverse(shard_rows):
        return jnp.dot(inverse_rows, shard_rows, preferred_element_type=jnp.float32)

    solved = apply_inverse(lax.all_gather(excite_rows, "sub", axis=0, tiled=True))
    solved_half = solved.astype(jnp.bfloat16)
    incident = lax.psum_scatter(
        lax.dot_general(
            solved_half, agg_columns, CONTRACT_FIRST, preferred_element_type=jnp.float32
        ).astype(jnp.bfloat16),
        "sub",
        scatter_dimension=0,
        tiled=True,
    ).astype(jnp.float32)
    spread = apply_inverse(lax.all_gather(disagg_rows, "sub", axis=0, tiled=True))
    spread_half = spread.astype(jnp.bfloat16)
    partial_map = lax.dot_general(
        spread_half, agg_columns, CONTRACT_FIRST, preferred_element_type=jnp.float32
    )
    coupling = lax.psum(partial_map.astype(jnp.bfloat16), "sub")
    domains = sweep_order.shape[0]
    segment_of = sweep_order * SEGMENTS // domains
    own_index = lax.axis_index("dom")
    my_segment = segment_of[own_index]
    slot_live = jnp.arange(partner_row.shape[0], dtype=jnp.int32) < list_counts[0]
    domain_ids = jnp.arange(domains, dtype=jnp.int32)
    incoming = jnp.zeros(incident.shape, jnp.float32)
    for segment_k in range(SEGMENTS - 1):
        pattern = (
            incident
            - jnp.dot(incoming.astype(jnp.bfloat16), coupling, preferred_element_type=jnp.float32)
        ).astype(jnp.bfloat16)
        pattern = jnp.where(my_segment == segment_k, pattern, jnp.zeros_like(pattern))
        make_piece = lax.all_gather(pattern[None], "dom", axis=0, tiled=True)
        count = make_piece.shape[0]
        make_senders = jnp.arange(count, dtype=jnp.int32)
        sender_segment = jnp.sum(
            jnp.where(domain_ids[None, :] == make_senders[:, None], segment_of[None, :], 0), axis=1
        )
        sender_live = sender_segment == segment_k
        match = (
            (partner_row[:, None] == make_senders[None, :])
            & slot_live[:, None]
            & sender_live[None, :]
            & (segment_k < my_segment)
        )
        weights = jnp.sum(
            jnp.where(match[:, :, None, None], trans_rows[:, None, :, :], 0.0), axis=0
        )
        terms = rotate(weights[:, 0][:, None, :], weights[:, 1][:, None, :], make_piece)
        incoming = incoming + jnp.sum(terms, axis=0)
    fields = lax.all_gather(incoming.astype(jnp.bfloat16), "sub", axis=0, tiled=True)
    currents = solved - lax.dot_general(
        spread_half, fields, CONTRACT_LAST, preferred_element_type=jnp.float32
    )
    return currents[None]


def solution(mesh):
    in_specs = (
        P("dom", "sub", None),
        P("dom", "sub", None),
        P("dom", None, "sub"),
        P("dom", "sub", None),
        P("dom", None, None, None),
        P("dom", None),
        P("dom"),
        P(),
    )
    out_specs = P("dom", "sub", None)
    return jax.shard_map(local, mesh=mesh, in_specs=in_specs, out_specs=out_specs, check_vma=False)
```

profile of v0, /device:TPU:8, one launch (start us, length us, event | category | flops | bytes accessed | tf_op | source)
XLA Modules:
  0.0 727.2 jit_solution(1331858626277878469)
XLA Ops:
  7.3 12.7 %all-gather = bf16[1,1536,64]{1,2,0:T(8,128)(2,1)S(1)} all-gather(bf16[1,384,64]{1,2,0:T(8,128)(2,1)} %param.8), channel_id=2, replica_groups=mesh['dom'=64,'sub'=4] {'sub'}, dimensions={1}, use_global_device_ids=true | all-gather | bytes 245760 | tf_op jit(solution)/shard_map/all_gather | solution.py:45
  22.2 31.2 %all-gather.18.cloned.1.call-done = bf16[1,1536,1024]{2,1,0:T(8,128)(2,1)} async-done(((bf16[1,384,1024]{2,1,0:T(8,128)(2,1)}), bf16[1,1536,1024]{2,1,0:T(8,128)(2,1)}) %all-gather.18.cloned.1.call-update) | async-done | bytes 3145744 | tf_op jit(solution)/shard_map/all_gather | solution.py:55
  53.4 3.3 fusion.2
  57.6 2.6 convolution_convert_fusion
  61.7 16.3 %reduce-scatter.2.cloned.1.call-done = bf16[16,1024]{1,0:T(8,128)(2,1)} async-done(((bf16[64,1024]{1,0:T(8,128)(2,1)}), bf16[16,1024]{1,0:T(8,128)(2,1)}) %reduce-scatter.2.cloned.1.call-update) | async-done | bytes 32784 | tf_op jit(solution)/shard_map/reduce_scatter | solution.py:47
  78.0 66.8 %all-reduce.2.cloned.1.call-done = bf16[1024,1024]{1,0:T(8,128)(2,1)} async-done(((bf16[1024,1024]{1,0:T(8,128)(2,1)}), bf16[1024,1024]{1,0:T(8,128)(2,1)}) %all-reduce.2.cloned.1.call-update) | async-done | bytes 2097168 | tf_op jit(solution)/shard_map/psum | solution.py:60
  144.8 2.6 fusion.10
  153.9 1.9 select_reduce_fusion
  155.8 70.0 %all-gather.20.cloned.1.call-done = bf16[1024,1024]{1,0:T(8,128)(2,1)} async-done(((bf16[16,1024]{1,0:T(8,128)(2,1)}), bf16[1024,1024]{1,0:T(8,128)(2,1)}) %all-gather.20.cloned.1.call-update) | async-done | bytes 2097168 | tf_op jit(solution)/shard_map/all_gather | solution.py:74
  225.8 2.1 convert
  232.0 1.7 slice_bitcast_fusion.11
  233.7 72.6 %all-gather.22.cloned.1.call-done = bf16[1024,1024]{1,0:T(8,128)(2,1)} async-done(((bf16[16,1024]{1,0:T(8,128)(2,1)}), bf16[1024,1024]{1,0:T(8,128)(2,1)}) %all-gather.22.cloned.1.call-update) | async-done | bytes 2097168 | tf_op jit(solution)/shard_map/all_gather | solution.py:74
  306.3 2.1 convert.1
  312.6 73.6 %all-gather.24.cloned.1.call-done = bf16[1024,1024]{1,0:T(8,128)(2,1)} async-done(((bf16[16,1024]{1,0:T(8,128)(2,1)}), bf16[1024,1024]{1,0:T(8,128)(2,1)}) %all-gather.24.cloned.1.call-update) | async-done | bytes 2097168 | tf_op jit(solution)/shard_map/all_gather | solution.py:74
  386.3 2.1 convert.2
  392.5 73.7 %all-gather.26.cloned.1.call-done = bf16[1024,1024]{1,0:T(8,128)(2,1)} async-done(((bf16[16,1024]{1,0:T(8,128)(2,1)}), bf16[1024,1024]{1,0:T(8,128)(2,1)}) %all-gather.26.cloned.1.call-update) | async-done | bytes 2097168 | tf_op jit(solution)/shard_map/all_gather | solution.py:74
  466.2 2.1 convert.3
  471.3 74.1 %all-gather.28.cloned.1.call-done = bf16[1024,1024]{1,0:T(8,128)(2,1)} async-done(((bf16[16,1024]{1,0:T(8,128)(2,1)}), bf16[1024,1024]{1,0:T(8,128)(2,1)}) %all-gather.28.cloned.1.call-update) | async-done | bytes 2097168 | tf_op jit(solution)/shard_map/all_gather | solution.py:74
  545.4 2.1 convert.4
  550.4 74.3 %all-gather.30.cloned.1.call-done = bf16[1024,1024]{1,0:T(8,128)(2,1)} async-done(((bf16[16,1024]{1,0:T(8,128)(2,1)}), bf16[1024,1024]{1,0:T(8,128)(2,1)}) %all-gather.30.cloned.1.call-update) | async-done | bytes 2097168 | tf_op jit(solution)/shard_map/all_gather | solution.py:74
  624.7 2.1 convert.5
  628.8 75.0 %all-gather.32.cloned.1.call-done = bf16[1024,1024]{1,0:T(8,128)(2,1)} async-done(((bf16[16,1024]{1,0:T(8,128)(2,1)}), bf16[1024,1024]{1,0:T(8,128)(2,1)}) %all-gather.32.cloned.1.call-update) | async-done | bytes 2097168 | tf_op jit(solution)/shard_map/all_gather | solution.py:74
  703.9 2.1 convert.6
  707.0 12.3 %all_gather.39 = bf16[64,1024]{1,0:T(8,128)(2,1)S(1)} all-gather(bf16[16,1024]{1,0:T(8,128)(2,1)S(1)} %add_convert_fusion), channel_id=1, replica_groups=mesh['dom'=64,'sub'=4] {'sub'}, dimensions={0}, use_global_device_ids=true | all-gather | bytes 163840 | tf_op jit(solution)/shard_map/all_gather | solution.py:92
  (99 shorter events, 23.6 us)
Async XLA Ops:
  6.5 13.4 %copy-start = (bf16[1,384,1536]{2,1,0:T(8,128)(2,1)S(1)}, bf16[1,384,1536]{2,1,0:T(8,128)(2,1)}, u32[]{:S(2)}) copy-start(bf16[1,384,1536]{2,1,0:T(8,128)(2,1)} %param.9) | copy-start | bytes 3538948
  6.5 14.6 %copy-start.8 = (bf16[1,1024,384]{2,1,0:T(8,128)(2,1)S(1)}, bf16[1,1024,384]{2,1,0:T(8,128)(2,1)}, u32[]{:S(2)}) copy-start(bf16[1,1024,384]{2,1,0:T(8,128)(2,1)} %param.10) | copy-start | bytes 2359300
  6.5 46.9 %all-gather.18.cloned.1.call-start = ((), (), s32[]{:S(2)}) async-start(), calls=%async_computation.3 | async-start | bytes 3932160 | tf_op jit(solution)/shard_map/all_gather | solution.py:55
  7.3 70.8 %reduce-scatter.2.cloned.1.call-start = ((), (), s32[]{:S(2)}) async-start(), calls=%async_computation.1 | async-start | bytes 163840 | tf_op jit(solution)/shard_map/reduce_scatter | solution.py:47
  22.2 122.6 %all-reduce.2.cloned.1.call-start = ((), (), s32[]{:S(2)}) async-start(), calls=%async_computation.2 | async-start | bytes 4194304 | tf_op jit(solution)/shard_map/psum | solution.py:60
  57.6 2.7 copy-start.18
  60.2 93.6 %copy-start.17 = (s32[1,6]{1,0:T(1,128)S(1)}, s32[1,6]{1,0:T(1,128)}, u32[]{:S(2)}) copy-start(s32[1,6]{1,0:T(1,128)} %param.13) | copy-start | bytes 76
  60.2 93.7 %copy-start.16 = (f32[1,6,2,512]{3,2,1,0:T(2,128)S(1)}, f32[1,6,2,512]{3,2,1,0:T(2,128)}, u32[]{:S(2)}) copy-start(f32[1,6,2,512]{3,2,1,0:T(2,128)} %param.12) | copy-start | bytes 73732
  60.2 165.5 %all-gather.20.cloned.1.call-start = ((), (), s32[]{:S(2)}) async-start(), calls=%async_computation.4 | async-start | bytes 2129920 | tf_op jit(solution)/shard_map/all_gather | solution.py:74
  147.4 158.9 %all-gather.22.cloned.1.call-start = ((), (), s32[]{:S(2)}) async-start(), calls=%async_computation.5 | async-start | bytes 2129920 | tf_op jit(solution)/shard_map/all_gather | solution.py:74
  228.6 1.6 copy-start.2
  231.3 155.0 %all-gather.24.cloned.1.call-start = ((), (), s32[]{:S(2)}) async-start(), calls=%async_computation.6 | async-start | bytes 2129920 | tf_op jit(solution)/shard_map/all_gather | solution.py:74
  306.3 2.1 copy-start.11
  306.3 2.1 copy-start.12
  311.2 155.0 %all-gather.26.cloned.1.call-start = ((), (), s32[]{:S(2)}) async-start(), calls=%async_computation.7 | async-start | bytes 2129920 | tf_op jit(solution)/shard_map/all_gather | solution.py:74
  386.3 2.1 copy-start.13
  386.3 2.1 copy-start.14
  391.1 154.3 %all-gather.28.cloned.1.call-start = ((), (), s32[]{:S(2)}) async-start(), calls=%async_computation.8 | async-start | bytes 2129920 | tf_op jit(solution)/shard_map/all_gather | solution.py:74
  466.2 2.1 copy-start.15
  470.4 154.3 %all-gather.30.cloned.1.call-start = ((), (), s32[]{:S(2)}) async-start(), calls=%async_computation.9 | async-start | bytes 2129920 | tf_op jit(solution)/shard_map/all_gather | solution.py:74
  549.6 154.3 %all-gather.32.cloned.1.call-start = ((), (), s32[]{:S(2)}) async-start(), calls=%async_computation.10 | async-start | bytes 2129920 | tf_op jit(solution)/shard_map/all_gather | solution.py:74
  706.8 13.6 %copy-start.1 = (bf16[1,384,1536]{2,1,0:T(8,128)(2,1)S(1)}, bf16[1,384,1536]{2,1,0:T(8,128)(2,1)}, u32[]{:S(2)}) copy-start(bf16[1,384,1536]{2,1,0:T(8,128)(2,1)} %param.9) | copy-start | bytes 3538948
  706.8 12.6 %copy-start.5 = (f32[384,64]{0,1:T(8,128)S(1)}, f32[384,64]{0,1:T(8,128)}, u32[]{:S(2)}) copy-start(f32[384,64]{0,1:T(8,128)} %copy-done.4) | copy-start | bytes 294916
  706.8 12.6 %copy-start.7 = (bf16[384,1024]{1,0:T(8,128)(2,1)S(1)}, bf16[384,1024]{1,0:T(8,128)(2,1)}, u32[]{:S(2)}) copy-start(bf16[384,1024]{1,0:T(8,128)(2,1)} %copy-done.6) | copy-start | bytes 2359300
  (5 other events, 4.6 us)
Sparse Core Ops, SparseCore 0:
  9.2 44.1 all-gather.17
  55.9 22.0 reduce-scatter.1
  80.5 64.2 all-reduce.1
  147.6 78.1 all-gather.19
  231.4 74.9 all-gather.21
  311.3 74.9 all-gather.23
  391.2 74.9 all-gather.25
  470.5 74.9 all-gather.27
  549.7 74.9 all-gather.29
  628.9 74.9 all-gather.31
where the time goes:
time: 728 us; the launch traced here: 727 us
  waiting for transfers between devices  629 us (86%)
  blocking collectives  25 us (3%)
  between operations  24.3 us (3%)
  other arithmetic  23.9 us (3%)
  matrix products  17 us (2%)
  local copies, waits for them, and re-layouts  7.96 us (1%)
    all_gather x7, waiting for transfers between devices, local(): make_piece = lax.all_gather(pattern[None], 'dom', axis=0, tiled=True)  513 us
    psum x1, waiting for transfers between devices, local(): coupling = lax.psum(partial_map.astype(jnp.bfloat16), 'sub')  66.8 us
    all_gather x1, waiting for transfers between devices, local(): lax.all_gather(disagg_rows, 'sub', axis=0, tiled=True)  31.2 us
    reduce_scatter x1, waiting for transfers between devices, local(): lax.psum_scatter(lax.dot_general(solved_half, agg_columns, CONTRACT_FIRST...  16.3 us
    convert_element_type x7, other arithmetic, rotate(): values = pattern.astype(jnp.float32)  14.6 us
  transfers between devices with their start and end apart: 10, of which 10 were waited for; matrix products, arithmetic and copies ran while one was open for 2% of the time, Pallas kernels for 0%

commit v1 on v0

--- a/solution.py
+++ b/solution.py
@@ -57,7 +57,7 @@
     partial_map = lax.dot_general(
         spread_half, agg_columns, CONTRACT_FIRST, preferred_element_type=jnp.float32
     )
-    coupling = lax.psum(partial_map.astype(jnp.bfloat16), "sub")
+    coupling = jnp.sum(lax.all_gather(partial_map.astype(jnp.bfloat16), "sub"), axis=0)
     domains = sweep_order.shape[0]
     segment_of = sweep_order * SEGMENTS // domains
     own_index = lax.axis_index("dom")

time: 728 us -> 755 us (1.037)
  waiting for transfers between devices: 629 us -> 652 us
    all_gather x0 -> x1, waiting for transfers between devices: none -> 72.6 us  [local(): lax.all_gather(partial_map.astype(jnp.bfloat16), 'sub')]
    psum x1 -> x0, waiting for transfers between devices: 66.8 us -> none  [local(): coupling = lax.psum(partial_map.astype(jnp.bfloat16), 'sub')]
    all_gather x1, waiting for transfers between devices: 31.2 us -> 46.1 us  [local(): lax.all_gather(disagg_rows, 'sub', axis=0, tiled=True)]
where the time goes in v1:
time: 755 us; the launch traced here: 754 us
  waiting for transfers between devices  652 us (86%)
  other arithmetic  30.5 us (4%)
  between operations  24.3 us (3%)
  blocking collectives  23.5 us (3%)
  matrix products  16.3 us (2%)
    all_gather x7, waiting for transfers between devices, local(): make_piece = lax.all_gather(pattern[None], 'dom', axis=0, tiled=True)  514 us
    all_gather x1, waiting for transfers between devices, local(): lax.all_gather(partial_map.astype(jnp.bfloat16), 'sub')  72.6 us
    all_gather x1, waiting for transfers between devices, local(): lax.all_gather(disagg_rows, 'sub', axis=0, tiled=True)  46.1 us
    reduce_scatter x1, waiting for transfers between devices, local(): lax.psum_scatter(lax.dot_general(solved_half, agg_columns, CONTRACT_FIRST...  18.1 us
  transfers between devices with their start and end apart: 10, of which 10 were waited for; matrix products, arithmetic and copies ran while one was open for 2% of the time, Pallas kernels for 0%

profile of v1, /device:TPU:8, one launch (start us, length us, event | category | flops | bytes accessed | tf_op | source)
XLA Modules:
  0.0 754.2 jit_solution(1682828596675708405)
XLA Ops:
  7.3 46.1 %all-gather.20.cloned.1.call-done = bf16[1,1536,1024]{2,1,0:T(8,128)(2,1)} async-done(((bf16[1,384,1024]{2,1,0:T(8,128)(2,1)}), bf16[1,1536,1024]{2,1,0:T(8,128)(2,1)}) %all-gather.20.cloned.1.call-update) | async-done | bytes 3145744 | tf_op jit(solution)/shard_map/all_gather | solution.py:55
  53.4 3.3 fusion.2
  56.7 2.7 convolution_convert_fusion
  59.5 11.2 %all-gather = bf16[1,1536,64]{1,2,0:T(8,128)(2,1)S(1)} all-gather(bf16[1,384,64]{1,2,0:T(8,128)(2,1)S(1)} %copy-done.17), channel_id=2, replica_groups=mesh['dom'=64,'sub'=4] {'sub'}, dimensions={1}, use_global_device_ids=true | all-gather | bytes 245760 | tf_op jit(solution)/shard_map/all_gather | solution.py:45
  73.7 72.6 %all-gather.22.cloned.1.call-done = bf16[4096,1024]{1,0:T(8,128)(2,1)} async-done(((bf16[1024,1024]{1,0:T(8,128)(2,1)}), bf16[4096,1024]{1,0:T(8,128)(2,1)}) %all-gather.22.cloned.1.call-update) | async-done | bytes 8388624 | tf_op jit(solution)/shard_map/all_gather | solution.py:60
  146.3 6.5 reduce_sum.148
  152.8 18.1 %reduce-scatter.2.cloned.1.call-done = bf16[16,1024]{1,0:T(8,128)(2,1)} async-done(((bf16[64,1024]{1,0:T(8,128)(2,1)}), bf16[16,1024]{1,0:T(8,128)(2,1)}) %reduce-scatter.2.cloned.1.call-update) | async-done | bytes 32784 | tf_op jit(solution)/shard_map/reduce_scatter | solution.py:47
  170.9 1.8 fusion.10
  179.2 1.9 select_reduce_fusion
  181.8 70.9 %all-gather.24.cloned.1.call-done = bf16[1024,1024]{1,0:T(8,128)(2,1)} async-done(((bf16[16,1024]{1,0:T(8,128)(2,1)}), bf16[1024,1024]{1,0:T(8,128)(2,1)}) %all-gather.24.cloned.1.call-update) | async-done | bytes 2097168 | tf_op jit(solution)/shard_map/all_gather | solution.py:74
  252.7 2.1 convert.1
  260.0 72.6 %all-gather.26.cloned.1.call-done = bf16[1024,1024]{1,0:T(8,128)(2,1)} async-done(((bf16[16,1024]{1,0:T(8,128)(2,1)}), bf16[1024,1024]{1,0:T(8,128)(2,1)}) %all-gather.26.cloned.1.call-update) | async-done | bytes 2097168 | tf_op jit(solution)/shard_map/all_gather | solution.py:74
  332.6 2.1 convert.2
  339.8 73.4 %all-gather.28.cloned.1.call-done = bf16[1024,1024]{1,0:T(8,128)(2,1)} async-done(((bf16[16,1024]{1,0:T(8,128)(2,1)}), bf16[1024,1024]{1,0:T(8,128)(2,1)}) %all-gather.28.cloned.1.call-update) | async-done | bytes 2097168 | tf_op jit(solution)/shard_map/all_gather | solution.py:74
  413.2 2.1 convert.3
  419.4 73.7 %all-gather.30.cloned.1.call-done = bf16[1024,1024]{1,0:T(8,128)(2,1)} async-done(((bf16[16,1024]{1,0:T(8,128)(2,1)}), bf16[1024,1024]{1,0:T(8,128)(2,1)}) %all-gather.30.cloned.1.call-update) | async-done | bytes 2097168 | tf_op jit(solution)/shard_map/all_gather | solution.py:74
  493.1 2.1 convert.4
  498.1 74.3 %all-gather.32.cloned.1.call-done = bf16[1024,1024]{1,0:T(8,128)(2,1)} async-done(((bf16[16,1024]{1,0:T(8,128)(2,1)}), bf16[1024,1024]{1,0:T(8,128)(2,1)}) %all-gather.32.cloned.1.call-update) | async-done | bytes 2097168 | tf_op jit(solution)/shard_map/all_gather | solution.py:74
  572.4 2.1 convert.5
  577.3 74.3 %all-gather.34.cloned.1.call-done = bf16[1024,1024]{1,0:T(8,128)(2,1)} async-done(((bf16[16,1024]{1,0:T(8,128)(2,1)}), bf16[1024,1024]{1,0:T(8,128)(2,1)}) %all-gather.34.cloned.1.call-update) | async-done | bytes 2097168 | tf_op jit(solution)/shard_map/all_gather | solution.py:74
  651.6 2.1 convert.6
  655.8 75.0 %all-gather.36.cloned.1.call-done = bf16[1024,1024]{1,0:T(8,128)(2,1)} async-done(((bf16[16,1024]{1,0:T(8,128)(2,1)}), bf16[1024,1024]{1,0:T(8,128)(2,1)}) %all-gather.36.cloned.1.call-update) | async-done | bytes 2097168 | tf_op jit(solution)/shard_map/all_gather | solution.py:74
  730.9 2.1 convert.7
  734.0 12.3 %all_gather.47 = bf16[64,1024]{1,0:T(8,128)(2,1)S(1)} all-gather(bf16[16,1024]{1,0:T(8,128)(2,1)S(1)} %add_convert_fusion), channel_id=1, replica_groups=mesh['dom'=64,'sub'=4] {'sub'}, dimensions={0}, use_global_device_ids=true | all-gather | bytes 163840 | tf_op jit(solution)/shard_map/all_gather | solution.py:92
  (104 shorter events, 24.5 us)
Async XLA Ops:
  6.5 46.9 %copy-start = (bf16[1,384,1536]{2,1,0:T(8,128)(2,1)S(1)}, bf16[1,384,1536]{2,1,0:T(8,128)(2,1)}, u32[]{:S(2)}) copy-start(bf16[1,384,1536]{2,1,0:T(8,128)(2,1)} %param.9) | copy-start | bytes 3538948
  6.5 46.9 %all-gather.20.cloned.1.call-start = ((), (), s32[]{:S(2)}) async-start(), calls=%async_computation.2 | async-start | bytes 3932160 | tf_op jit(solution)/shard_map/all_gather | solution.py:55
  7.3 49.4 %copy-start.5 = (bf16[1,1024,384]{2,1,0:T(8,128)(2,1)S(1)}, bf16[1,1024,384]{2,1,0:T(8,128)(2,1)}, u32[]{:S(2)}) copy-start(bf16[1,1024,384]{2,1,0:T(8,128)(2,1)} %param.10) | copy-start | bytes 2359300
  7.3 139.0 %all-gather.22.cloned.1.call-start = ((), (), s32[]{:S(2)}) async-start(), calls=%async_computation.3 | async-start | bytes 10485760 | tf_op jit(solution)/shard_map/all_gather | solution.py:60
  56.7 2.7 copy-start.3
  56.7 2.8 copy-start.17
  59.4 12.9 %copy-start.20 = (s32[64]{0:T(128)S(1)}, s32[64]{0:T(128)}, u32[]{:S(2)}) copy-start(s32[64]{0:T(128)} %param.15) | copy-start | bytes 772
  59.4 111.5 %reduce-scatter.2.cloned.1.call-start = ((), (), s32[]{:S(2)}) async-start(), calls=%async_computation.1 | async-start | bytes 163840 | tf_op jit(solution)/shard_map/reduce_scatter | solution.py:47
  72.2 180.5 %all-gather.24.cloned.1.call-start = ((), (), s32[]{:S(2)}) async-start(), calls=%async_computation.4 | async-start | bytes 2129920 | tf_op jit(solution)/shard_map/all_gather | solution.py:74
  152.8 26.3 %copy-start.19 = (s32[1,6]{1,0:T(1,128)S(1)}, s32[1,6]{1,0:T(1,128)}, u32[]{:S(2)}) copy-start(s32[1,6]{1,0:T(1,128)} %param.13) | copy-start | bytes 76
  152.8 26.4 %copy-start.18 = (f32[1,6,2,512]{3,2,1,0:T(2,128)S(1)}, f32[1,6,2,512]{3,2,1,0:T(2,128)}, u32[]{:S(2)}) copy-start(f32[1,6,2,512]{3,2,1,0:T(2,128)} %param.12) | copy-start | bytes 73732
  172.7 159.9 %all-gather.26.cloned.1.call-start = ((), (), s32[]{:S(2)}) async-start(), calls=%async_computation.5 | async-start | bytes 2129920 | tf_op jit(solution)/shard_map/all_gather | solution.py:74
  252.7 2.1 copy-start.10
  252.7 2.1 copy-start.11
  257.6 155.6 %all-gather.28.cloned.1.call-start = ((), (), s32[]{:S(2)}) async-start(), calls=%async_computation.6 | async-start | bytes 2129920 | tf_op jit(solution)/shard_map/all_gather | solution.py:74
  332.6 2.1 copy-start.12
  332.6 2.1 copy-start.13
  338.1 155.0 %all-gather.30.cloned.1.call-start = ((), (), s32[]{:S(2)}) async-start(), calls=%async_computation.7 | async-start | bytes 2129920 | tf_op jit(solution)/shard_map/all_gather | solution.py:74
  413.2 2.1 copy-start.15
  418.0 154.4 %all-gather.32.cloned.1.call-start = ((), (), s32[]{:S(2)}) async-start(), calls=%async_computation.8 | async-start | bytes 2129920 | tf_op jit(solution)/shard_map/all_gather | solution.py:74
  497.3 154.3 %all-gather.34.cloned.1.call-start = ((), (), s32[]{:S(2)}) async-start(), calls=%async_computation.9 | async-start | bytes 2129920 | tf_op jit(solution)/shard_map/all_gather | solution.py:74
  576.5 154.3 %all-gather.36.cloned.1.call-start = ((), (), s32[]{:S(2)}) async-start(), calls=%async_computation.10 | async-start | bytes 2129920 | tf_op jit(solution)/shard_map/all_gather | solution.py:74
  733.7 13.6 %copy-start.1 = (bf16[1,384,1536]{2,1,0:T(8,128)(2,1)S(1)}, bf16[1,384,1536]{2,1,0:T(8,128)(2,1)}, u32[]{:S(2)}) copy-start(bf16[1,384,1536]{2,1,0:T(8,128)(2,1)} %param.9) | copy-start | bytes 3538948
  733.7 12.6 %copy-start.4 = (bf16[384,1024]{1,0:T(8,128)(2,1)S(1)}, bf16[384,1024]{1,0:T(8,128)(2,1)}, u32[]{:S(2)}) copy-start(bf16[384,1024]{1,0:T(8,128)(2,1)} %copy-done.3) | copy-start | bytes 2359300
  (7 other events, 8.1 us)
Sparse Core Ops, SparseCore 0:
  9.2 44.1 all-gather.19
  59.5 86.6 all-gather.21
  148.8 22.0 reduce-scatter.1
  173.9 78.7 all-gather.23
  257.7 74.9 all-gather.25
  338.2 74.9 all-gather.27
  418.1 74.9 all-gather.29
  497.4 74.9 all-gather.31
  576.7 74.9 all-gather.33
  655.9 74.9 all-gather.35
